TPU v7x, 32 devices: a whole 2x2x4 slice. The times are simulated.
32 devices in a mesh: region: 8 (over y, x, core), dom: 4 (over z).
Axes of the slice: x: 2, y: 2, z: 4, core: 2. Of those that a mesh axis runs over, the one named last changes fastest.
Arguments:
- feats: bfloat16 [16384, 512], P(('region', 'dom')), may hold values from -6 to 6
- hub_feats: bfloat16 [64, 512], P('region'), may hold values from -6 to 6
- hub_ids: int32 [16384, 4], P(('region', 'dom')), may hold values from 0 to 63
- tile_src: int32 [512], P(('region', 'dom')), may hold values from 0 to 4
- tile_mask: int32 [512, 128, 128], P(('region', 'dom')), may hold values 0 or 1
- w_stack: bfloat16 [1024, 512], replicated, may hold values from -0.1875 to 0.1875
- cotangent: bfloat16 [16384, 512], P(('region', 'dom')), may hold values from -6 to 6
Outputs:
- activ: bfloat16 [16384, 512], P(('region', 'dom'))
- weight_grad: float32 [1024, 512], P('dom')
- hub_grad: float32 [64, 512], P('region')
Inputs may be any that keep to these rules, and one draw needn't show every extreme that they name: tile_src names a block of the part's window: 0 is the block taken from the previous part, 1 to 4 are the part's own blocks. `hub_ids`: hub ids index rows of hub_feats.
All inputs are finite; a program needn't handle non-finite values. No bound on the sum of `tile_mask` on one device may be relied on, other than what follows from the above.
Results may differ from a plain program's by a relative error of at most 0.0051.
Values may be sent and summed in bfloat16 or wider, within the bound.
No kernel may reach another device: no remote copies, remote signals or barrier semaphores. Data moves between devices by JAX's collectives and lax.ppermute only.
A program may use at most 64 MiB of HBM per device.

v0:
```python
import jax
import jax.numpy as jnp
from jax import lax
from jax.sharding import PartitionSpec as P


def shifted(value, axis, steps):
    count = lax.axis_size(axis)
    initial, last = (max(0, -steps), min(count, count - steps))
    return lax.ppermute(value, axis, [(source, source + steps) for source in range(initial, last)])


def on_device(feats, hub_feats, hub_ids, tile_src, tile_mask, w_stack, cotangent):
    rows, width = feats.shape
    tile = tile_mask.shape[1]
    nblk = rows // tile
    per_block = tile_src.shape[0] // nblk
    hub_count = hub_ids.shape[1]
    owned = hub_feats.shape[0]
    total_hubs = owned * lax.axis_size("region")
    prev = shifted(feats[rows - tile :], "dom", 1)
    window = jnp.concatenate([prev, feats], axis=0).reshape(nblk + 1, tile, width)
    picked = jnp.take(window, tile_src, axis=0)
    mask_b = tile_mask.astype(jnp.bfloat16)
    prod = jnp.einsum("tij,tjd->tid", mask_b, picked, preferred_element_type=jnp.float32)
    nsum = prod.reshape(nblk, per_block, tile, width).sum(axis=1).reshape(rows, width)
    cnt = tile_mask.reshape(nblk, per_block, tile, tile).sum(axis=(1, 3)).reshape(rows)
    deg = 1.0 + cnt.astype(jnp.float32) + jnp.float32(hub_count)
    hub_cols = lax.broadcasted_iota(jnp.int32, (rows, total_hubs), 1)
    counts = jnp.zeros((rows, total_hubs), jnp.float32)
    for slot in range(hub_count):
        counts = counts + (hub_ids[:, slot : slot + 1] == hub_cols).astype(jnp.float32)
    counts = counts.astype(jnp.bfloat16)
    block = counts
    hsum = jnp.dot(
        block,
        lax.all_gather(hub_feats, "region", axis=0, tiled=True),
        preferred_element_type=jnp.float32,
    )
    agg = ((feats.astype(jnp.float32) + nsum + hsum) / deg[:, None]).astype(jnp.bfloat16)
    inputs = jnp.concatenate([feats, agg], axis=1)
    z = jnp.dot(inputs, w_stack, preferred_element_type=jnp.float32)
    sig = jax.nn.sigmoid(z)
    activ = (z * sig).astype(jnp.bfloat16)
    dz = (cotangent.astype(jnp.float32) * sig * (1.0 + z * (1.0 - sig))).astype(jnp.bfloat16)
    partial_w = lax.psum_scatter(
        lax.dot_general(inputs, dz, (((0,), (0,)), ((), ())), preferred_element_type=jnp.float32),
        "dom",
        scatter_dimension=0,
        tiled=True,
    )
    weight_grad = lax.psum(partial_w, "region")
    dagg = lax.dot_general(
        dz, w_stack[width:], (((1,), (1,)), ((), ())), preferred_element_type=jnp.float32
    )
    sgrad = (dagg / deg[:, None]).astype(jnp.bfloat16)
    block = counts
    region_sum = lax.psum_scatter(
        lax.dot_general(block, sgrad, (((0,), (0,)), ((), ())), preferred_element_type=jnp.float32),
        "region",
        scatter_dimension=0,
        tiled=True,
    )
    hub_grad = lax.psum(region_sum, "dom")
    return (activ, weight_grad, hub_grad)


def solution(mesh):
    placed = (
        P(("region", "dom"), None),
        P("region", None),
        P(("region", "dom"), None),
        P(("region", "dom")),
        P(("region", "dom"), None, None),
        P(),
        P(("region", "dom"), None),
    )
    return jax.shard_map(
        on_device,
        mesh=mesh,
        in_specs=placed,
        out_specs=(P(("region", "dom"), None), P("dom", None), P("region", None)),
        check_vma=False,
    )
```

profile of v0, /device:TPU:0, one launch (start us, length us, event | category | flops | bytes accessed | tf_op | source)
XLA Modules:
  0.0 183.3 jit_solution(3585333480241991576)
XLA Ops:
  7.2 0.0 reduce-scatter.3.cloned.1.call-start
  7.2 1.0 slice.18
  8.2 5.0 %collective-permute-start = (bf16[128,512]{1,0:T(8,128)(2,1)S(1)}, bf16[128,512]{1,0:T(8,128)(2,1)S(1)}, u32[]{:S(2)}, u32[]{:S(2)}) collective-permute-start(bf16[128,512]{1,0:T(8,128)(2,1)S(1)} %slice.18), channel_id=1, source_target_pairs={{0,1},{1,2},{2,3},{4,5},{5,6},{6,7},{8,9},{9,10},{10,11},{12,13},{... | collective-permute-start | bytes 393224 | tf_op jit(solution)/shard_map/ppermute | solution.py:10
  13.2 1.6 reduce_sum.26
  14.8 0.9 fusion.19
  15.6 0.7 compare_select_fusion
  16.3 0.7 compare_and_fusion
  17.0 1.3 copy.23
  18.2 9.3 %all_gather.3 = bf16[64,512]{1,0:T(8,128)(2,1)S(1)} all-gather(bf16[8,512]{1,0:T(8,128)(2,1)S(1)} %copy-done.2), channel_id=1, replica_groups=mesh['region'=8,'dom'=4] {'region'}, dimensions={0}, use_global_device_ids=true | all-gather | bytes 73728 | tf_op jit(solution)/shard_map/all_gather | solution.py:37
  27.6 2.0 %gather_fusion = bf16[16,128,512]{2,1,0:T(8,128)(2,1)} fusion(bf16[5,128,512]{2,1,0:T(8,128)(2,1)S(1)} %bitcast.23, s32[1024]{0:T(1024)S(1)} %pad_clamp_fusion), kind=kCustom, calls=%fused_computation | custom fusion | bytes 4194368 | tf_op jit(solution)/shard_map/jit(_take)/gather | solution.py:23
  29.6 2.6 %bitcast_reduce_fusion = f32[4,128,512]{1,2,0:T(8,128)S(1)} fusion(bf16[16,128,512]{2,1,0:T(8,128)(2,1)} %gather_fusion, pred[16]{0:T(512)(128)(4,1)S(1)} %compare_and_fusion, s32[16,128,128]{2,1,0:T(8,128)S(1)} %copy-done.1), kind=kOutput, calls=%fused_computation.1 | convolution fusion | flops 270532608 | bytes 4194320 | tf_op jit(solution)/shard_map/tij,tjd->tid/dot_general | solution.py:25
  32.2 1.0 fusion.6
  33.2 0.2 copy-done.3
  33.4 0.1 copy-done.4
  33.6 1.9 %multiply_convert_fusion = (bf16[512,512]{1,0:T(8,128)(2,1)S(1)}, bf16[512,512]{1,0:T(8,128)(2,1)}) fusion(bf16[512,512]{1,0:T(8,128)(2,1)S(1)} %copy-done.4, bf16[1024,512]{1,0:T(8,128)(2,1)S(1)} %copy-done.3, bf16[512,512]{0,1:T(8,128)(2,1)S(1)} %fusion.6, bf16[512,512]{0,1:T(8,128)(2,1)S(1)} %copy.23), kind=kOutput, calls=%fused_computation.13 | convolution fusion | flops 542113792 | bytes 3670016 | tf_op jit(solution)/shard_map/dot_general | solution.py:42
  35.5 2.1 %fusion.10 = f32[1024,512]{1,0:T(8,128)} fusion(bf16[512,512]{1,0:T(8,128)(2,1)S(1)} %get-tuple-element.3, bf16[512,512]{0,1:T(8,128)(2,1)S(1)} %fusion.6, bf16[512,512]{0,1:T(8,128)(2,1)S(1)} %copy.23), kind=kOutput, calls=%fused_computation.17 | convolution fusion | flops 538968064 | bytes 3670016 | tf_op jit(solution)/shard_map/dot_general | solution.py:47
  37.6 0.0 reduce-scatter.5.cloned.1.call-start
  37.6 1.3 fusion.8
  39.0 0.0 all-reduce.2.cloned.1.call-start
  39.0 41.6 %reduce-scatter.3.cloned.1.call-done = f32[256,512]{1,0:T(8,128)} async-done(((f32[1024,512]{1,0:T(8,128)}), f32[256,512]{1,0:T(8,128)}) %reduce-scatter.3.cloned.1.call-update) | async-done | bytes 524304 | tf_op jit(solution)/shard_map/reduce_scatter | solution.py:46
  80.7 36.3 %reduce-scatter.5.cloned.1.call-done = f32[8,512]{1,0:T(8,128)} async-done(((f32[64,512]{1,0:T(8,128)}), f32[8,512]{1,0:T(8,128)}) %reduce-scatter.5.cloned.1.call-update) | async-done | bytes 16400 | tf_op jit(solution)/shard_map/reduce_scatter | solution.py:58
  117.0 19.9 %psum.15 = f32[8,512]{1,0:T(8,128)} all-reduce(f32[8,512]{1,0:T(8,128)} %reduce-scatter.5.cloned.1.call-done), channel_id=1, replica_groups=mesh['region'=8,'dom'=4] {'dom'}, use_global_device_ids=true, to_apply=%region_6.7 | all-reduce | flops 4096 | bytes 32768 | tf_op jit(solution)/shard_map/psum | solution.py:64
  136.9 38.0 %all-reduce.2.cloned.1.call-done = f32[256,512]{1,0:T(8,128)} async-done(((f32[256,512]{1,0:T(8,128)}), f32[256,512]{1,0:T(8,128)}) %all-reduce.2.cloned.1.call-update) | async-done | bytes 524304 | tf_op jit(solution)/shard_map/psum | solution.py:52
  174.9 1.9 %copy.30 = f32[256,512]{1,0:T(8,128)} copy(f32[256,512]{1,0:T(8,128)} %all-reduce.2.cloned.1.call-done) | data formatting | bytes 1048576
  (16 shorter events, 0.2 us)
Async XLA Ops:
  7.2 20.3 %copy-start = (bf16[512,512]{1,0:T(8,128)(2,1)S(1)}, bf16[512,512]{1,0:T(8,128)(2,1)}, u32[]{:S(2)}) copy-start(bf16[512,512]{1,0:T(8,128)(2,1)} %param.7) | copy-start | bytes 1572868
  7.2 11.0 %copy-start.2 = (bf16[8,512]{1,0:T(8,128)(2,1)S(1)}, bf16[8,512]{1,0:T(8,128)(2,1)}, u32[]{:S(2)}) copy-start(bf16[8,512]{1,0:T(8,128)(2,1)} %param.8) | copy-start | bytes 24580
  7.2 73.4 %reduce-scatter.3.cloned.1.call-start = ((), (), s32[]{:S(2)}) async-start(), calls=%async_computation.2 | async-start | bytes 2621440 | tf_op jit(solution)/shard_map/reduce_scatter | solution.py:46
  8.2 19.3 %collective-permute-start = (bf16[128,512]{1,0:T(8,128)(2,1)S(1)}, bf16[128,512]{1,0:T(8,128)(2,1)S(1)}, u32[]{:S(2)}, u32[]{:S(2)}) collective-permute-start(bf16[128,512]{1,0:T(8,128)(2,1)S(1)} %slice.18), channel_id=1, source_target_pairs={{0,1},{1,2},{2,3},{4,5},{5,6},{6,7},{8,9},{9,10},{10,11},{12,13},{... | collective-permute-start | bytes 393224 | tf_op jit(solution)/shard_map/ppermute | solution.py:10
  27.6 2.0 %copy-start.1 = (s32[16,128,128]{2,1,0:T(8,128)S(1)}, s32[16,128,128]{2,1,0:T(8,128)}, u32[]{:S(2)}) copy-start(s32[16,128,128]{2,1,0:T(8,128)} %param.11) | copy-start | bytes 3145732
  32.2 1.2 copy-start.3
  32.2 1.3 copy-start.4
  37.6 79.4 %reduce-scatter.5.cloned.1.call-start = ((), (), s32[]{:S(2)}) async-start(), calls=%async_computation.4 | async-start | bytes 147456 | tf_op jit(solution)/shard_map/reduce_scatter | solution.py:58
  39.0 135.9 %all-reduce.2.cloned.1.call-start = ((), (), s32[]{:S(2)}) async-start(), calls=%async_computation.3 | async-start | bytes 1048576 | tf_op jit(solution)/shard_map/psum | solution.py:52
Sparse Core Ops, SparseCore 0:
  37.7 42.8 reduce-scatter.2
  84.2 32.7 reduce-scatter.4
  120.1 54.7 all-reduce.1
where the time goes:
time: 184 us; the launch traced here: 183 us
  waiting for transfers between devices  116 us (63%)
  blocking collectives  29.2 us (16%)
  between operations  13.9 us (8%)
  matrix products  8.9 us (5%)
  local copies, waits for them, and re-layouts  7.35 us (4%)
  starting transfers between devices  5.08 us (3%)
  other arithmetic  2.97 us (2%)
    reduce_scatter x1, waiting for transfers between devices, on_device(): lax.psum_scatter(lax.dot_general(inputs, dz, (((0,), (0,)), ((), ())), pr...  41.6 us
    psum x1, waiting for transfers between devices, on_device(): weight_grad = lax.psum(partial_w, 'region')  38 us
    reduce_scatter x1, waiting for transfers between devices, on_device(): lax.psum_scatter(lax.dot_general(block, sgrad, (((0,), (0,)), ((), ())),...  36.3 us
    psum x1, blocking collectives, on_device(): hub_grad = lax.psum(region_sum, 'dom')  19.9 us
    all_gather x1, blocking collectives, on_device(): lax.all_gather(hub_feats, 'region', axis=0, tiled=True)  9.26 us
    ppermute x1, starting transfers between devices, shifted(): lax.ppermute(value, axis, [(source, source + steps) for source in range(i...  4.96 us
  transfers between devices with their start and end apart: 4, of which 3 were waited for; matrix products, arithmetic and copies ran while one was open for 3% of the time, Pallas kernels for 0%

commit v1 on v0

--- a/solution.py
+++ b/solution.py
@@ -49,7 +49,7 @@
         scatter_dimension=0,
         tiled=True,
     )
-    weight_grad = lax.psum(partial_w, "region")
+    weight_grad = jnp.sum(lax.all_gather(partial_w, "region"), axis=0)
     dagg = lax.dot_general(
         dz, w_stack[width:], (((1,), (1,)), ((), ())), preferred_element_type=jnp.float32
     )

time: 184 us -> 166 us (0.902)
  waiting for transfers between devices: 116 us -> 96.5 us
  other arithmetic: 2.97 us -> 6.45 us
  local copies, waits for them, and re-layouts: 7.35 us -> 5.48 us
    psum x1 -> x0, waiting for transfers between devices: 38 us -> none  [on_device(): weight_grad = lax.psum(partial_w, 'region')]
    all_gather x0 -> x1, waiting for transfers between devices: none -> 18.6 us  [on_device(): weight_grad = jnp.sum(lax.all_gather(partial_w, 'region'), axis=0)]
    reduce_sum x0 -> x1, other arithmetic: none -> 3.49 us  [on_device(): weight_grad = jnp.sum(lax.all_gather(partial_w, 'region'), axis=0)]
    unnamed x12 -> x11, local copies, waits for them, and re-layouts: 3.5 us -> 1.63 us
  transfers between devices with their start and end apart: 4 -> 4, of which waited for: 3 -> 3; matrix products, arithmetic and copies ran while one was open for 3% -> 4% of each run, Pallas kernels for 0% -> 0%
where the time goes in v1:
time: 166 us
  waiting for transfers between devices  96.5 us (58%)
  blocking collectives  29.2 us (18%)
  between operations  13.9 us (8%)
  matrix products  8.9 us (5%)
  other arithmetic  6.45 us (4%)
  local copies, waits for them, and re-layouts  5.48 us (3%)
  starting transfers between devices  5.08 us (3%)
    reduce_scatter x1, waiting for transfers between devices, on_device(): lax.psum_scatter(lax.dot_general(inputs, dz, (((0,), (0,)), ((), ())), pr...  41.6 us
    reduce_scatter x1, waiting for transfers between devices, on_device(): lax.psum_scatter(lax.dot_general(block, sgrad, (((0,), (0,)), ((), ())),...  36.3 us
    psum x1, blocking collectives, on_device(): hub_grad = lax.psum(region_sum, 'dom')  19.9 us
    all_gather x1, waiting for transfers between devices, on_device(): weight_grad = jnp.sum(lax.all_gather(partial_w, 'region'), axis=0)  18.6 us
    all_gather x1, blocking collectives, on_device(): lax.all_gather(hub_feats, 'region', axis=0, tiled=True)  9.26 us
    ppermute x1, starting transfers between devices, shifted(): lax.ppermute(value, axis, [(source, source + steps) for source in range(i...  4.96 us
    reduce_sum x1, other arithmetic, on_device(): weight_grad = jnp.sum(lax.all_gather(partial_w, 'region'), axis=0)  3.49 us
  transfers between devices with their start and end apart: 4, of which 3 were waited for; matrix products, arithmetic and copies ran while one was open for 4% of the time, Pallas kernels for 0%

profile of v1, /device:TPU:0, one launch (start us, length us, event | category | flops | bytes accessed | tf_op | source)
XLA Modules:
  0.0 165.5 jit_solution(13485696315172568815)
XLA Ops:
  7.2 0.0 reduce-scatter.3.cloned.1.call-start
  7.2 1.0 slice.18
  8.2 5.0 %collective-permute-start = (bf16[128,512]{1,0:T(8,128)(2,1)S(1)}, bf16[128,512]{1,0:T(8,128)(2,1)S(1)}, u32[]{:S(2)}, u32[]{:S(2)}) collective-permute-start(bf16[128,512]{1,0:T(8,128)(2,1)S(1)} %slice.18), channel_id=1, source_target_pairs={{0,1},{1,2},{2,3},{4,5},{5,6},{6,7},{8,9},{9,10},{10,11},{12,13},{... | collective-permute-start | bytes 393224 | tf_op jit(solution)/shard_map/ppermute | solution.py:10
  13.2 0.7 compare_and_fusion
  13.8 1.6 reduce_sum.35
  15.4 0.9 fusion.19
  16.3 0.7 compare_select_fusion
  17.0 1.3 copy.23
  18.2 9.3 %all_gather.9 = bf16[64,512]{1,0:T(8,128)(2,1)S(1)} all-gather(bf16[8,512]{1,0:T(8,128)(2,1)S(1)} %copy-done.2), channel_id=1, replica_groups=mesh['region'=8,'dom'=4] {'region'}, dimensions={0}, use_global_device_ids=true | all-gather | bytes 73728 | tf_op jit(solution)/shard_map/all_gather | solution.py:37
  27.6 2.0 %gather_fusion = bf16[16,128,512]{2,1,0:T(8,128)(2,1)} fusion(bf16[5,128,512]{2,1,0:T(8,128)(2,1)S(1)} %bitcast.24, s32[1024]{0:T(1024)S(1)} %pad_clamp_fusion), kind=kCustom, calls=%fused_computation | custom fusion | bytes 4194368 | tf_op jit(solution)/shard_map/jit(_take)/gather | solution.py:23
  29.6 2.6 %bitcast_reduce_fusion = f32[4,128,512]{1,2,0:T(8,128)S(1)} fusion(bf16[16,128,512]{2,1,0:T(8,128)(2,1)} %gather_fusion, pred[16]{0:T(512)(128)(4,1)S(1)} %compare_and_fusion, s32[16,128,128]{2,1,0:T(8,128)S(1)} %copy-done.1), kind=kOutput, calls=%fused_computation.1 | convolution fusion | flops 270532608 | bytes 4194320 | tf_op jit(solution)/shard_map/tij,tjd->tid/dot_general | solution.py:25
  32.2 1.0 fusion.6
  33.2 0.2 copy-done.3
  33.5 0.1 copy-done.4
  33.6 1.9 %multiply_convert_fusion = (bf16[512,512]{1,0:T(8,128)(2,1)S(1)}, bf16[512,512]{1,0:T(8,128)(2,1)}) fusion(bf16[512,512]{1,0:T(8,128)(2,1)S(1)} %copy-done.4, bf16[1024,512]{1,0:T(8,128)(2,1)S(1)} %copy-done.3, bf16[512,512]{0,1:T(8,128)(2,1)S(1)} %fusion.6, bf16[512,512]{0,1:T(8,128)(2,1)S(1)} %copy.23), kind=kOutput, calls=%fused_computation.13 | convolution fusion | flops 542113792 | bytes 3670016 | tf_op jit(solution)/shard_map/dot_general | solution.py:42
  35.5 2.1 %fusion.10 = f32[1024,512]{1,0:T(8,128)} fusion(bf16[512,512]{1,0:T(8,128)(2,1)S(1)} %get-tuple-element.3, bf16[512,512]{0,1:T(8,128)(2,1)S(1)} %fusion.6, bf16[512,512]{0,1:T(8,128)(2,1)S(1)} %copy.23), kind=kOutput, calls=%fused_computation.17 | convolution fusion | flops 538968064 | bytes 3670016 | tf_op jit(solution)/shard_map/dot_general | solution.py:47
  37.6 0.0 reduce-scatter.5.cloned.1.call-start
  37.6 1.3 fusion.8
  39.0 0.0 all-gather.3.cloned.1.call-start
  39.0 41.6 %reduce-scatter.3.cloned.1.call-done = f32[256,512]{1,0:T(8,128)} async-done(((f32[1024,512]{1,0:T(8,128)}), f32[256,512]{1,0:T(8,128)}) %reduce-scatter.3.cloned.1.call-update) | async-done | bytes 524304 | tf_op jit(solution)/shard_map/reduce_scatter | solution.py:46
  80.7 36.3 %reduce-scatter.5.cloned.1.call-done = f32[8,512]{1,0:T(8,128)} async-done(((f32[64,512]{1,0:T(8,128)}), f32[8,512]{1,0:T(8,128)}) %reduce-scatter.5.cloned.1.call-update) | async-done | bytes 16400 | tf_op jit(solution)/shard_map/reduce_scatter | solution.py:58
  117.0 19.9 %psum.7 = f32[8,512]{1,0:T(8,128)} all-reduce(f32[8,512]{1,0:T(8,128)} %reduce-scatter.5.cloned.1.call-done), channel_id=1, replica_groups=mesh['region'=8,'dom'=4] {'dom'}, use_global_device_ids=true, to_apply=%region_6.7 | all-reduce | flops 4096 | bytes 32768 | tf_op jit(solution)/shard_map/psum | solution.py:64
  136.9 18.6 %all-gather.3.cloned.1.call-done = f32[2048,512]{1,0:T(8,128)} async-done(((f32[256,512]{1,0:T(8,128)}), f32[2048,512]{1,0:T(8,128)}) %all-gather.3.cloned.1.call-update) | async-done | bytes 4194320 | tf_op jit(solution)/shard_map/all_gather | solution.py:52
  155.5 3.5 %reduce_sum.38 = f32[256,512]{1,0:T(8,128)} reduce(f32[8,256,512]{2,1,0:T(8,128)} %bitcast.25, f32[]{:T(128)} %constant.22.clone.1), dimensions={0}, to_apply=%region_4.5 | reduce | flops 917504 | bytes 4718596 | tf_op jit(solution)/shard_map/reduce_sum | solution.py:52
  (16 shorter events, 0.2 us)
Async XLA Ops:
  7.2 20.3 %copy-start = (bf16[512,512]{1,0:T(8,128)(2,1)S(1)}, bf16[512,512]{1,0:T(8,128)(2,1)}, u32[]{:S(2)}) copy-start(bf16[512,512]{1,0:T(8,128)(2,1)} %param.7) | copy-start | bytes 1572868
  7.2 11.0 %copy-start.2 = (bf16[8,512]{1,0:T(8,128)(2,1)S(1)}, bf16[8,512]{1,0:T(8,128)(2,1)}, u32[]{:S(2)}) copy-start(bf16[8,512]{1,0:T(8,128)(2,1)} %param.8) | copy-start | bytes 24580
  7.2 73.4 %reduce-scatter.3.cloned.1.call-start = ((), (), s32[]{:S(2)}) async-start(), calls=%async_computation.2 | async-start | bytes 2621440 | tf_op jit(solution)/shard_map/reduce_scatter | solution.py:46
  8.2 19.3 %collective-permute-start = (bf16[128,512]{1,0:T(8,128)(2,1)S(1)}, bf16[128,512]{1,0:T(8,128)(2,1)S(1)}, u32[]{:S(2)}, u32[]{:S(2)}) collective-permute-start(bf16[128,512]{1,0:T(8,128)(2,1)S(1)} %slice.18), channel_id=1, source_target_pairs={{0,1},{1,2},{2,3},{4,5},{5,6},{6,7},{8,9},{9,10},{10,11},{12,13},{... | collective-permute-start | bytes 393224 | tf_op jit(solution)/shard_map/ppermute | solution.py:10
  27.6 2.0 %copy-start.1 = (s32[16,128,128]{2,1,0:T(8,128)S(1)}, s32[16,128,128]{2,1,0:T(8,128)}, u32[]{:S(2)}) copy-start(s32[16,128,128]{2,1,0:T(8,128)} %param.11) | copy-start | bytes 3145732
  32.2 1.2 copy-start.3
  32.2 1.3 copy-start.4
  37.6 79.4 %reduce-scatter.5.cloned.1.call-start = ((), (), s32[]{:S(2)}) async-start(), calls=%async_computation.3 | async-start | bytes 147456 | tf_op jit(solution)/shard_map/reduce_scatter | solution.py:58
  39.0 116.5 %all-gather.3.cloned.1.call-start = ((), (), s32[]{:S(2)}) async-start(), calls=%async_computation.4 | async-start | bytes 4718592 | tf_op jit(solution)/shard_map/all_gather | solution.py:52
Sparse Core Ops, SparseCore 0:
  37.7 42.8 reduce-scatter.2
  84.2 32.7 reduce-scatter.4
  118.9 36.5 all-gather.2
